TPU v7x, 32 devices: a whole 2x2x4 slice. The times are simulated.
32 devices in a mesh: ep: 16 (over z, y, core), dp: 2 (over x).
Axes of the slice: x: 2, y: 2, z: 4, core: 2. Of those that a mesh axis runs over, the one named last changes fastest.
Arguments:
- moe_rows: bfloat16 [1024, 3584], P(('dp', 'ep')), parts along dimension 0, may hold values from -6 to 6
- routes: int32 [1024, 4], P(('dp', 'ep')), parts along dimension 0, may hold values from 0 to 7, all different within a row; in each aligned block of 32 rows (0 to 31, 32 to 63, ...) at most 32 rows name the same one
- route_weights: float32 [1024, 4], P(('dp', 'ep')), parts along dimension 0, may hold values from 0.05 to 0.5
- w_gate: bfloat16 [16, 3584, 512], P('ep'), may hold values from -0.09375 to 0.09375
- w_up: bfloat16 [16, 3584, 512], P('ep'), may hold values from -0.09375 to 0.09375
- w_down: bfloat16 [16, 512, 3584], P('ep'), may hold values from -0.1875 to 0.1875
- queries: bfloat16 [128, 64, 576], P(('dp', 'ep')), parts along dimension 0, may hold values from -45 to 45
- latent_cache: bfloat16 [128, 128, 576], P(('dp', 'ep')), parts along dimension 0, may hold values from -6 to 6
- lengths: int32 [128], P(('dp', 'ep')), parts along dimension 0, may hold values from 2 to 128, as said below
Outputs:
- moe_out: bfloat16 [1024, 3584], P(('dp', 'ep')), parts along dimension 0
- attn_out: bfloat16 [128, 64, 512], P(('dp', 'ep')), parts along dimension 0
There are 2 independent parts, one for each index of `dp`. A program takes and returns all parts, laid end to end along the dimension named above; an argument that names none is the same for every part. Nothing has to cross between parts.
Inputs may be any that keep to these rules, and one draw needn't show every extreme that they name: `routes`: each row names 4 different experts; in each aligned block of 32 rows (the rows of one device) no expert is named by more than 32 rows, a bound that some block reaches. `lengths`: some row of every part uses all 128 positions.
All inputs are finite; a program needn't handle non-finite values.
Results may differ from a plain program's by a relative error of at most 0.0085.
Values may be sent and summed in bfloat16 or wider, within the bound.
No kernel may reach another device: no remote copies, remote signals or barrier semaphores. Data moves between devices by JAX's collectives and lax.ppermute only.
A program may use at most 128 MiB of HBM per device.

v0:
```python
import jax
import jax.numpy as jnp
from jax import lax
from jax.sharding import PartitionSpec as P

LATENT = 512
score_scale = 192.0 ** (-0.5)


def attend(queries, latent_cache, lengths):
    scores = (
        jnp.einsum("rhc,rlc->rhl", queries, latent_cache, preferred_element_type=jnp.float32)
        * score_scale
    )
    in_range = (
        jnp.arange(latent_cache.shape[1], dtype=jnp.int32)[None, None, :] < lengths[:, None, None]
    )
    scores = jnp.where(in_range, scores, -1e30)
    highest = jnp.max(scores, axis=-1, keepdims=True)
    expo = jnp.where(in_range, jnp.exp(scores - highest), 0.0)
    probs = (expo / jnp.sum(expo, axis=-1, keepdims=True)).astype(jnp.bfloat16)
    return jnp.einsum(
        "rhl,rlc->rhc", probs, latent_cache[:, :, :LATENT], preferred_element_type=jnp.float32
    ).astype(jnp.bfloat16)


def shards(moe_rows, routes, route_weights, w_gate, w_up, w_down, queries, latent_cache, lengths):
    attn_out = attend(queries, latent_cache, lengths)
    rows_here, model_width = moe_rows.shape
    picks = routes.shape[1]
    devices = lax.axis_size("ep")
    experts = devices // 2
    capacity = min(rows_here, 2 * rows_here * picks // experts)
    flat_experts = routes.reshape(-1)
    matches = (flat_experts[:, None] == jnp.arange(experts, dtype=jnp.int32)[None, :]).astype(
        jnp.int32
    )
    before = jnp.cumsum(matches, axis=0) - matches
    slot_index = jnp.sum(before * matches, axis=1)
    target = flat_experts * capacity + slot_index
    source_rows = jnp.repeat(moe_rows, picks, axis=0)
    packed = jnp.zeros((experts * capacity, model_width), jnp.bfloat16).at[target].set(source_rows)
    packed = packed.reshape(experts, capacity, model_width)
    outgoing = jnp.repeat(packed, 2, axis=0)
    received = lax.all_to_all(outgoing, "ep", split_axis=0, concat_axis=0, tiled=True)
    senders = received.shape[0]
    item_count = received.shape[1]
    flat_rows = received.reshape(-1, model_width)
    gate_act = jnp.dot(flat_rows, w_gate[0], preferred_element_type=jnp.float32)
    up_act = jnp.dot(flat_rows, w_up[0], preferred_element_type=jnp.float32)
    hidden = (jax.nn.silu(gate_act) * up_act).astype(jnp.bfloat16)
    partial_out = jnp.dot(hidden, w_down[0], preferred_element_type=jnp.float32)
    returned = lax.all_to_all(
        partial_out.reshape(senders, item_count, model_width),
        "ep",
        split_axis=0,
        concat_axis=0,
        tiled=True,
    )
    expert_out = jnp.sum(returned.reshape(experts, 2, capacity, model_width), axis=1).astype(
        jnp.bfloat16
    )
    slot_out = expert_out.reshape(experts * capacity, model_width)[target]
    slot_out = slot_out.reshape(rows_here, picks, model_width)
    moe_out = jnp.einsum(
        "rk,rkd->rd", route_weights, slot_out, preferred_element_type=jnp.float32
    ).astype(jnp.bfloat16)
    return (moe_out, attn_out)


def solution(mesh):
    in_specs = (
        P(("dp", "ep"), None),
        P(("dp", "ep"), None),
        P(("dp", "ep"), None),
        P("ep", None, None),
        P("ep", None, None),
        P("ep", None, None),
        P(("dp", "ep"), None, None),
        P(("dp", "ep"), None, None),
        P(("dp", "ep")),
    )
    out_specs = (P(("dp", "ep"), None), P(("dp", "ep"), None, None))
    return jax.shard_map(shards, mesh=mesh, in_specs=in_specs, out_specs=out_specs, check_vma=False)
```

profile of v0, /device:TPU:13, one launch (start us, length us, event | category | flops | bytes accessed | tf_op | source)
XLA Modules:
  0.0 276.1 jit_solution(15898886306179961386)
XLA Ops:
  0.6 0.0 copy-start
  0.6 0.8 copy.15
  1.5 0.7 broadcast_multiply_fusion
  2.1 0.1 eq.15
  2.2 0.1 fusion.21
  2.3 0.2 reduce_window_sum.11
  2.5 0.2 select_reduce_fusion
  2.7 0.1 copy.14
  2.8 0.1 mul.34
  2.9 1.2 broadcast_in_dim.35
  4.1 0.2 reshape.98
  4.3 2.5 scatter_custom_fusion
  6.8 0.4 broadcast_in_dim.36
  7.1 0.0 copy-start.4
  7.2 87.6 %all_to_all.10 = bf16[16,32,3584]{2,1,0:T(8,128)(2,1)S(1)} all-to-all(bf16[16,32,3584]{2,1,0:T(8,128)(2,1)S(1)} %bitcast.41), channel_id=1, replica_groups=mesh['ep'=16,'dp'=2] {'ep'}, dimensions={0} | all-to-all | bytes 7340032 | tf_op jit(solution)/shard_map/all_to_all | solution.py:45
  94.8 0.0 copy-done.4
  94.8 0.0 copy-start.5
  94.8 2.0 fusion.5
  96.8 0.0 copy-done.5
  96.8 0.0 copy-start.1
  96.9 2.1 fusion.10
  99.0 0.0 copy-done.1
  99.0 5.1 %fusion.1 = f32[16,32,3584]{2,1,0:T(8,128)} fusion(bf16[16,32,512]{2,1,0:T(8,128)(2,1)S(1)} %bitcast.45, bf16[1,512,3584]{2,1,0:T(8,128)(2,1)S(1)} %copy-done.1), kind=kOutput, calls=%fused_computation.4 | convolution fusion | flops 1879048192 | bytes 11534336 | tf_op jit(solution)/shard_map/dot_general | solution.py:52
  104.1 0.0 copy-start.3
  104.1 0.0 copy-start.6
  104.1 0.0 copy-start.2
  104.1 5.4 %all-to-all-start.1 = ((f32[16,32,3584]{2,1,0:T(8,128)}), f32[16,32,3584]{2,1,0:T(8,128)}, u32[]{:S(2)}, u32[]{:S(2)}) async-start(f32[16,32,3584]{2,1,0:T(8,128)} %fusion.1), calls=%async_computation.1 | async-start | bytes 14680064 | tf_op jit(solution)/shard_map/all_to_all | solution.py:53
  109.5 0.0 copy-done.3
  109.5 0.1 copy.17
  109.6 0.0 copy-done.6
  109.6 0.1 iota_compare_fusion.1
  109.7 0.0 copy-done
  109.7 0.0 copy-done.2
  109.7 0.2 fusion.14
  110.0 0.2 fusion.25
  110.2 1.3 convolution_convert_fusion
  111.4 157.9 %all-to-all-done.1 = f32[16,32,3584]{2,1,0:T(8,128)} async-done(((f32[16,32,3584]{2,1,0:T(8,128)}), f32[16,32,3584]{2,1,0:T(8,128)}, u32[]{:S(2)}, u32[]{:S(2)}) %all-to-all-start.1) | async-done | bytes 7340064 | tf_op jit(solution)/shard_map/all_to_all | solution.py:53
  269.4 4.1 %bitcast_reduce_fusion = bf16[8,32,3584]{2,1,0:T(8,128)(2,1)S(1)} fusion(f32[16,32,3584]{2,1,0:T(8,128)} %all-to-all-done.1), kind=kLoop, calls=%fused_computation.3 | loop fusion | flops 917504 | bytes 9175040 | tf_op jit(solution)/shard_map/reduce_sum | solution.py:60
  273.5 1.1 gather_fusion
  274.6 0.2 reshape.85
  274.8 0.6 fusion.26
  275.4 0.7 copy.21
  (2 shorter events, 0.0 us)
Async XLA Ops:
  0.6 109.1 %copy-start = (bf16[4,64,576]{2,1,0:T(8,128)(2,1)S(1)}, bf16[4,64,576]{2,1,0:T(8,128)(2,1)}, u32[]{:S(2)}) copy-start(bf16[4,64,576]{2,1,0:T(8,128)(2,1)} %param.15) | copy-start | bytes 884740
  7.1 87.6 %copy-start.4 = (bf16[1,3584,512]{2,1,0:T(8,128)(2,1)S(1)}, bf16[1,3584,512]{2,1,0:T(8,128)(2,1)}, u32[]{:S(2)}) copy-start(bf16[1,3584,512]{2,1,0:T(8,128)(2,1)} %param.12) | copy-start | bytes 11010052
  94.8 2.1 copy-start.5
  96.8 2.2 copy-start.1
  104.1 5.4 %copy-start.3 = (f32[32,4]{0,1:T(4,128)S(1)}, f32[32,4]{0,1:T(4,128)}, u32[]{:S(2)}) copy-start(f32[32,4]{0,1:T(4,128)} %param.11) | copy-start | bytes 1540
  104.1 5.5 %copy-start.6 = (s32[4]{0:T(128)S(1)}, s32[4]{0:T(128)}, u32[]{:S(2)}) copy-start(s32[4]{0:T(128)} %param.17) | copy-start | bytes 52
  104.1 5.6 %copy-start.2 = (bf16[4,128,576]{1,2,0:T(8,128)(2,1)S(1)}, bf16[4,128,576]{1,2,0:T(8,128)(2,1)}, u32[]{:S(2)}) copy-start(bf16[4,128,576]{1,2,0:T(8,128)(2,1)} %param.16) | copy-start | bytes 1769476
  104.1 165.2 %all-to-all-start.1 = ((f32[16,32,3584]{2,1,0:T(8,128)}), f32[16,32,3584]{2,1,0:T(8,128)}, u32[]{:S(2)}, u32[]{:S(2)}) async-start(f32[16,32,3584]{2,1,0:T(8,128)} %fusion.1), calls=%async_computation.1 | async-start | bytes 14680064 | tf_op jit(solution)/shard_map/all_to_all | solution.py:53
where the time goes:
time: 276 us
  waiting for transfers between devices  158 us (57%)
  blocking collectives  87.6 us (32%)
  matrix products  11.5 us (4%)
  local copies, waits for them, and re-layouts  7.5 us (3%)
  other arithmetic  5.47 us (2%)
  starting transfers between devices  5.37 us (2%)
    all_to_all x1, waiting for transfers between devices, shards(): lax.all_to_all(partial_out.reshape(senders, item_count, model_width), 'ep...  158 us
    all_to_all x1, blocking collectives, shards(): lax.all_to_all(outgoing, 'ep', split_axis=0, concat_axis=0, tiled=True)  87.6 us
  transfers between devices with their start and end apart: 1, of which 1 were waited for; matrix products, arithmetic and copies ran while one was open for 1% of the time, Pallas kernels for 0%

commit v1 on v0

--- a/solution.py
+++ b/solution.py
@@ -5,6 +5,26 @@
 
 LATENT = 512
 score_scale = 192.0 ** (-0.5)
+
+
+def save_object(panel, row_axis):
+    later, met_up = (jax.lax.axis_size(row_axis), jax.lax.axis_index(row_axis))
+    even = list(panel.shape)
+    opened = panel.shape[0] // later
+    even[0] = opened
+    low = even[0]
+    even[0] = low * later
+    m = 0
+    r1 = jnp.zeros(even, panel.dtype)
+    while m < later:
+        base_arr = lax.dynamic_slice_in_dim(panel, (met_up ^ m) * opened, opened, axis=0)
+        if m:
+            base_arr = jax.lax.ppermute(
+                base_arr, axis_name=row_axis, perm=[(idx, idx ^ m) for idx in range(later)]
+            )
+        r1 = lax.dynamic_update_slice_in_dim(r1, base_arr, (met_up ^ m) * low, axis=0)
+        m += 1
+    return r1
 
 
 def attend(queries, latent_cache, lengths):
@@ -42,7 +62,7 @@
     packed = jnp.zeros((experts * capacity, model_width), jnp.bfloat16).at[target].set(source_rows)
     packed = packed.reshape(experts, capacity, model_width)
     outgoing = jnp.repeat(packed, 2, axis=0)
-    received = lax.all_to_all(outgoing, "ep", split_axis=0, concat_axis=0, tiled=True)
+    received = save_object(outgoing, "ep")
     senders = received.shape[0]
     item_count = received.shape[1]
     flat_rows = received.reshape(-1, model_width)

time: 276 us -> 286 us (1.036)
  blocking collectives: 87.6 us -> 0 us
  waiting for transfers between devices: 158 us -> 235 us
  starting transfers between devices: 5.37 us -> 23.3 us
    all_to_all x1 -> x0, blocking collectives: 87.6 us -> none  [shards(): lax.all_to_all(outgoing, 'ep', split_axis=0, concat_axis=0, tiled=True)]
    ppermute x0 -> x15, waiting for transfers between devices: none -> 77.1 us  [save_object(): jax.lax.ppermute(base_arr, axis_name=row_axis, perm=[(idx, idx ^ m) for i...]
    ppermute x0 -> x15, starting transfers between devices: none -> 17 us  [save_object(): jax.lax.ppermute(base_arr, axis_name=row_axis, perm=[(idx, idx ^ m) for i...]
  transfers between devices with their start and end apart: 1 -> 16, of which waited for: 1 -> 12; matrix products, arithmetic and copies ran while one was open for 1% -> 1% of each run, Pallas kernels for 0% -> 0%
where the time goes in v1:
time: 286 us; the launch traced here: 285 us
  waiting for transfers between devices  235 us (82%)
  starting transfers between devices  23.3 us (8%)
  matrix products  11.4 us (4%)
  local copies, waits for them, and re-layouts  8.46 us (3%)
  other arithmetic  5.47 us (2%)
    all_to_all x1, waiting for transfers between devices, shards(): lax.all_to_all(partial_out.reshape(senders, item_count, model_width), 'ep...  158 us
    ppermute x15, waiting for transfers between devices, save_object(): jax.lax.ppermute(base_arr, axis_name=row_axis, perm=[(idx, idx ^ m) for i...  77.1 us
    ppermute x15, starting transfers between devices, save_object(): jax.lax.ppermute(base_arr, axis_name=row_axis, perm=[(idx, idx ^ m) for i...  17 us
    all_to_all x1, starting transfers between devices, shards(): lax.all_to_all(partial_out.reshape(senders, item_count, model_width), 'ep...  6.3 us
  transfers between devices with their start and end apart: 16, of which 12 were waited for; matrix products, arithmetic and copies ran while one was open for 1% of the time, Pallas kernels for 0%

profile of v1, /device:TPU:13, one launch (start us, length us, event | category | flops | bytes accessed | tf_op | source)
XLA Modules:
  0.0 285.2 jit_solution(14965492920136115958)
XLA Ops:
  0.6 0.0 copy-start
  0.7 0.8 copy.15
  1.5 0.7 broadcast_multiply_fusion
  2.2 0.1 eq.15
  2.3 0.1 fusion.15
  2.4 0.2 reduce_window_sum.11
  2.6 0.2 select_reduce_fusion
  2.7 0.1 copy.14
  2.8 0.1 mul.34
  2.9 1.2 broadcast_in_dim.39
  4.1 0.2 reshape.98
  4.4 2.5 scatter_custom_fusion
  6.9 0.4 broadcast_in_dim.40
  7.3 0.3 broadcast_in_dim.37
  7.6 0.3 constant_dynamic-slice_fusion.14
  8.0 0.0 copy-start.4
  8.0 0.7 collective-permute-start
  8.7 0.2 collective-permute-start.1
  9.0 1.5 collective-permute-start.2
  10.5 0.2 collective-permute-start.3
  10.6 1.6 collective-permute-start.4
  12.3 0.0 collective-permute-done
  12.3 0.0 collective-permute-start.5
  12.3 3.6 %collective-permute-done.1 = bf16[1,32,3584]{2,1,0:T(8,128)(2,1)S(1)} collective-permute-done((bf16[1,32,3584]{2,1,0:T(8,128)(2,1)S(1)}, bf16[1,32,3584]{2,1,0:T(8,128)(2,1)S(1)}, u32[]{:S(2)}, u32[]{:S(2)}) %collective-permute-start.1) | collective-permute-done | bytes 229408 | tf_op jit(solution)/shard_map/ppermute | solution.py:22
  15.9 0.9 collective-permute-start.6
  16.8 4.5 %collective-permute-done.2 = bf16[1,32,3584]{2,1,0:T(8,128)(2,1)S(1)} collective-permute-done((bf16[1,32,3584]{2,1,0:T(8,128)(2,1)S(1)}, bf16[1,32,3584]{2,1,0:T(8,128)(2,1)S(1)}, u32[]{:S(2)}, u32[]{:S(2)}) %collective-permute-start.2) | collective-permute-done | bytes 229408 | tf_op jit(solution)/shard_map/ppermute | solution.py:22
  21.3 2.3 collective-permute-start.7
  23.6 0.0 collective-permute-done.3
  23.6 0.2 collective-permute-start.8
  23.9 0.0 collective-permute-done.4
  23.9 2.3 collective-permute-start.9
  26.2 9.1 %collective-permute-done.5 = bf16[1,32,3584]{2,1,0:T(8,128)(2,1)S(1)} collective-permute-done((bf16[1,32,3584]{2,1,0:T(8,128)(2,1)S(1)}, bf16[1,32,3584]{2,1,0:T(8,128)(2,1)S(1)}, u32[]{:S(2)}, u32[]{:S(2)}) %collective-permute-start.5) | collective-permute-done | bytes 229408 | tf_op jit(solution)/shard_map/ppermute | solution.py:22
  35.3 4.4 %collective-permute-start.10 = (bf16[1,32,3584]{2,1,0:T(8,128)(2,1)S(1)}, bf16[1,32,3584]{2,1,0:T(8,128)(2,1)S(1)}, u32[]{:S(2)}, u32[]{:S(2)}) collective-permute-start(bf16[1,32,3584]{2,1,0:T(8,128)(2,1)S(1)} %get-tuple-element.6), channel_id=1, source_target_pairs={{0,22},{2,20},{4,18},{6,16},{8,30},{10,28},{12,26},{14,24},{16,6},... | collective-permute-start | bytes 688136 | tf_op jit(solution)/shard_map/ppermute | solution.py:22
  39.7 0.5 collective-permute-done.6
  40.2 0.9 collective-permute-start.11
  41.1 0.0 collective-permute-done.7
  41.1 1.8 collective-permute-start.12
  42.9 20.2 %collective-permute-done.8 = bf16[1,32,3584]{2,1,0:T(8,128)(2,1)S(1)} collective-permute-done((bf16[1,32,3584]{2,1,0:T(8,128)(2,1)S(1)}, bf16[1,32,3584]{2,1,0:T(8,128)(2,1)S(1)}, u32[]{:S(2)}, u32[]{:S(2)}) %collective-permute-start.8) | collective-permute-done | bytes 229408 | tf_op jit(solution)/shard_map/ppermute | solution.py:22
  63.2 0.0 collective-permute-start.13
  63.2 4.9 %collective-permute-done.9 = bf16[1,32,3584]{2,1,0:T(8,128)(2,1)S(1)} collective-permute-done((bf16[1,32,3584]{2,1,0:T(8,128)(2,1)S(1)}, bf16[1,32,3584]{2,1,0:T(8,128)(2,1)S(1)}, u32[]{:S(2)}, u32[]{:S(2)}) %collective-permute-start.9) | collective-permute-done | bytes 229408 | tf_op jit(solution)/shard_map/ppermute | solution.py:22
  68.1 0.0 collective-permute-start.14
  68.1 9.8 %collective-permute-done.10 = bf16[1,32,3584]{2,1,0:T(8,128)(2,1)S(1)} collective-permute-done((bf16[1,32,3584]{2,1,0:T(8,128)(2,1)S(1)}, bf16[1,32,3584]{2,1,0:T(8,128)(2,1)S(1)}, u32[]{:S(2)}, u32[]{:S(2)}) %collective-permute-start.10) | collective-permute-done | bytes 229408 | tf_op jit(solution)/shard_map/ppermute | solution.py:22
  77.9 9.8 %collective-permute-done.11 = bf16[1,32,3584]{2,1,0:T(8,128)(2,1)S(1)} collective-permute-done((bf16[1,32,3584]{2,1,0:T(8,128)(2,1)S(1)}, bf16[1,32,3584]{2,1,0:T(8,128)(2,1)S(1)}, u32[]{:S(2)}, u32[]{:S(2)}) %collective-permute-start.11) | collective-permute-done | bytes 229408 | tf_op jit(solution)/shard_map/ppermute | solution.py:22
  87.8 5.3 %collective-permute-done.12 = bf16[1,32,3584]{2,1,0:T(8,128)(2,1)S(1)} collective-permute-done((bf16[1,32,3584]{2,1,0:T(8,128)(2,1)S(1)}, bf16[1,32,3584]{2,1,0:T(8,128)(2,1)S(1)}, u32[]{:S(2)}, u32[]{:S(2)}) %collective-permute-start.12) | collective-permute-done | bytes 229408 | tf_op jit(solution)/shard_map/ppermute | solution.py:22
  93.1 4.5 %collective-permute-done.13 = bf16[1,32,3584]{2,1,0:T(8,128)(2,1)S(1)} collective-permute-done((bf16[1,32,3584]{2,1,0:T(8,128)(2,1)S(1)}, bf16[1,32,3584]{2,1,0:T(8,128)(2,1)S(1)}, u32[]{:S(2)}, u32[]{:S(2)}) %collective-permute-start.13) | collective-permute-done | bytes 229408 | tf_op jit(solution)/shard_map/ppermute | solution.py:22
  97.6 4.9 %collective-permute-done.14 = bf16[1,32,3584]{2,1,0:T(8,128)(2,1)S(1)} collective-permute-done((bf16[1,32,3584]{2,1,0:T(8,128)(2,1)S(1)}, bf16[1,32,3584]{2,1,0:T(8,128)(2,1)S(1)}, u32[]{:S(2)}, u32[]{:S(2)}) %collective-permute-start.14) | collective-permute-done | bytes 229408 | tf_op jit(solution)/shard_map/ppermute | solution.py:22
  102.5 0.0 copy-start.5
  102.5 2.1 fusion.5
  104.6 0.0 copy-start.1
  104.6 2.1 multiply_convert_fusion
  106.8 0.0 copy-done.1
  106.8 5.1 %fusion.1 = f32[16,32,3584]{2,1,0:T(8,128)} fusion(bf16[16,32,512]{2,1,0:T(8,128)(2,1)S(1)} %bitcast.43, bf16[1,512,3584]{2,1,0:T(8,128)(2,1)S(1)} %copy-done.1), kind=kOutput, calls=%fused_computation.4 | convolution fusion | flops 1879048192 | bytes 11534336 | tf_op jit(solution)/shard_map/dot_general | solution.py:72
  111.9 6.3 %all-to-all-start = ((f32[16,32,3584]{2,1,0:T(8,128)}), f32[16,32,3584]{2,1,0:T(8,128)}, u32[]{:S(2)}, u32[]{:S(2)}) async-start(f32[16,32,3584]{2,1,0:T(8,128)} %fusion.1), calls=%async_computation | async-start | bytes 14680064 | tf_op jit(solution)/shard_map/all_to_all | solution.py:73
  118.2 0.1 copy.17
  118.3 0.1 iota_compare_fusion.1
  118.4 0.2 fusion.8
  118.6 0.2 fusion.19
  118.8 1.3 convolution_convert_fusion
  120.1 158.3 %all-to-all-done = f32[16,32,3584]{2,1,0:T(8,128)} async-done(((f32[16,32,3584]{2,1,0:T(8,128)}), f32[16,32,3584]{2,1,0:T(8,128)}, u32[]{:S(2)}, u32[]{:S(2)}) %all-to-all-start) | async-done | bytes 7340064 | tf_op jit(solution)/shard_map/all_to_all | solution.py:73
  278.4 4.1 %bitcast_reduce_fusion = bf16[8,32,3584]{2,1,0:T(8,128)(2,1)S(1)} fusion(f32[16,32,3584]{2,1,0:T(8,128)} %all-to-all-done), kind=kLoop, calls=%fused_computation.3 | loop fusion | flops 917504 | bytes 9175040 | tf_op jit(solution)/shard_map/reduce_sum | solution.py:80
  282.5 1.1 gather_fusion
  283.6 0.2 reshape.85
  283.9 0.6 fusion.20
  284.5 0.7 copy.21
  (26 shorter events, 0.3 us)
Async XLA Ops:
  0.6 117.7 %copy-start = (bf16[4,64,576]{2,1,0:T(8,128)(2,1)S(1)}, bf16[4,64,576]{2,1,0:T(8,128)(2,1)}, u32[]{:S(2)}) copy-start(bf16[4,64,576]{2,1,0:T(8,128)(2,1)} %param.15) | copy-start | bytes 884740
  8.0 94.5 %copy-start.4 = (bf16[1,3584,512]{2,1,0:T(8,128)(2,1)S(1)}, bf16[1,3584,512]{2,1,0:T(8,128)(2,1)}, u32[]{:S(2)}) copy-start(bf16[1,3584,512]{2,1,0:T(8,128)(2,1)} %param.12) | copy-start | bytes 11010052
  8.0 4.3 %collective-permute-start = (bf16[1,32,3584]{2,1,0:T(8,128)(2,1)S(1)}, bf16[1,32,3584]{2,1,0:T(8,128)(2,1)S(1)}, u32[]{:S(2)}, u32[]{:S(2)}) collective-permute-start(bf16[1,32,3584]{2,1,0:T(8,128)(2,1)S(1)} %get-tuple-element.16), channel_id=1, source_target_pairs={{0,2},{2,0},{4,6},{6,4},{8,10},{10,8},{12,14},{14,12},{16,18},{18,... | collective-permute-start | bytes 688136 | tf_op jit(solution)/shard_map/ppermute | solution.py:22
  8.7 7.2 %collective-permute-start.1 = (bf16[1,32,3584]{2,1,0:T(8,128)(2,1)S(1)}, bf16[1,32,3584]{2,1,0:T(8,128)(2,1)S(1)}, u32[]{:S(2)}, u32[]{:S(2)}) collective-permute-start(bf16[1,32,3584]{2,1,0:T(8,128)(2,1)S(1)} %get-tuple-element.15), channel_id=1, source_target_pairs={{0,4},{2,6},{4,0},{6,2},{8,12},{10,14},{12,8},{14,10},{16,20},{18,... | collective-permute-start | bytes 688136 | tf_op jit(solution)/shard_map/ppermute | solution.py:22
  9.0 12.3 %collective-permute-start.2 = (bf16[1,32,3584]{2,1,0:T(8,128)(2,1)S(1)}, bf16[1,32,3584]{2,1,0:T(8,128)(2,1)S(1)}, u32[]{:S(2)}, u32[]{:S(2)}) collective-permute-start(bf16[1,32,3584]{2,1,0:T(8,128)(2,1)S(1)} %get-tuple-element.14), channel_id=1, source_target_pairs={{0,6},{2,4},{4,2},{6,0},{8,14},{10,12},{12,10},{14,8},{16,22},{18,... | collective-permute-start | bytes 688136 | tf_op jit(solution)/shard_map/ppermute | solution.py:22
  10.5 13.2 %collective-permute-start.3 = (bf16[1,32,3584]{2,1,0:T(8,128)(2,1)S(1)}, bf16[1,32,3584]{2,1,0:T(8,128)(2,1)S(1)}, u32[]{:S(2)}, u32[]{:S(2)}) collective-permute-start(bf16[1,32,3584]{2,1,0:T(8,128)(2,1)S(1)} %get-tuple-element.13), channel_id=1, source_target_pairs={{0,8},{2,10},{4,12},{6,14},{8,0},{10,2},{12,4},{14,6},{16,24},{18,... | collective-permute-start | bytes 688136 | tf_op jit(solution)/shard_map/ppermute | solution.py:22
  10.6 13.3 %collective-permute-start.4 = (bf16[1,32,3584]{2,1,0:T(8,128)(2,1)S(1)}, bf16[1,32,3584]{2,1,0:T(8,128)(2,1)S(1)}, u32[]{:S(2)}, u32[]{:S(2)}) collective-permute-start(bf16[1,32,3584]{2,1,0:T(8,128)(2,1)S(1)} %get-tuple-element.12), channel_id=1, source_target_pairs={{0,10},{2,8},{4,14},{6,12},{8,2},{10,0},{12,6},{14,4},{16,26},{18,... | collective-permute-start | bytes 688136 | tf_op jit(solution)/shard_map/ppermute | solution.py:22
  12.3 23.1 %collective-permute-start.5 = (bf16[1,32,3584]{2,1,0:T(8,128)(2,1)S(1)}, bf16[1,32,3584]{2,1,0:T(8,128)(2,1)S(1)}, u32[]{:S(2)}, u32[]{:S(2)}) collective-permute-start(bf16[1,32,3584]{2,1,0:T(8,128)(2,1)S(1)} %get-tuple-element.11), channel_id=1, source_target_pairs={{0,12},{2,14},{4,8},{6,10},{8,4},{10,6},{12,0},{14,2},{16,28},{18,... | collective-permute-start | bytes 688136 | tf_op jit(solution)/shard_map/ppermute | solution.py:22
  15.9 24.3 %collective-permute-start.6 = (bf16[1,32,3584]{2,1,0:T(8,128)(2,1)S(1)}, bf16[1,32,3584]{2,1,0:T(8,128)(2,1)S(1)}, u32[]{:S(2)}, u32[]{:S(2)}) collective-permute-start(bf16[1,32,3584]{2,1,0:T(8,128)(2,1)S(1)} %get-tuple-element.10), channel_id=1, source_target_pairs={{0,14},{2,12},{4,10},{6,8},{8,6},{10,4},{12,2},{14,0},{16,30},{18,... | collective-permute-start | bytes 688136 | tf_op jit(solution)/shard_map/ppermute | solution.py:22
  21.3 19.8 %collective-permute-start.7 = (bf16[1,32,3584]{2,1,0:T(8,128)(2,1)S(1)}, bf16[1,32,3584]{2,1,0:T(8,128)(2,1)S(1)}, u32[]{:S(2)}, u32[]{:S(2)}) collective-permute-start(bf16[1,32,3584]{2,1,0:T(8,128)(2,1)S(1)} %get-tuple-element.9), channel_id=1, source_target_pairs={{0,16},{2,18},{4,20},{6,22},{8,24},{10,26},{12,28},{14,30},{16,0},... | collective-permute-start | bytes 688136 | tf_op jit(solution)/shard_map/ppermute | solution.py:22
  23.6 39.5 %collective-permute-start.8 = (bf16[1,32,3584]{2,1,0:T(8,128)(2,1)S(1)}, bf16[1,32,3584]{2,1,0:T(8,128)(2,1)S(1)}, u32[]{:S(2)}, u32[]{:S(2)}) collective-permute-start(bf16[1,32,3584]{2,1,0:T(8,128)(2,1)S(1)} %get-tuple-element.8), channel_id=1, source_target_pairs={{0,18},{2,16},{4,22},{6,20},{8,26},{10,24},{12,30},{14,28},{16,2},... | collective-permute-start | bytes 688136 | tf_op jit(solution)/shard_map/ppermute | solution.py:22
  23.9 44.2 %collective-permute-start.9 = (bf16[1,32,3584]{2,1,0:T(8,128)(2,1)S(1)}, bf16[1,32,3584]{2,1,0:T(8,128)(2,1)S(1)}, u32[]{:S(2)}, u32[]{:S(2)}) collective-permute-start(bf16[1,32,3584]{2,1,0:T(8,128)(2,1)S(1)} %get-tuple-element.7), channel_id=1, source_target_pairs={{0,20},{2,22},{4,16},{6,18},{8,28},{10,30},{12,24},{14,26},{16,4},... | collective-permute-start | bytes 688136 | tf_op jit(solution)/shard_map/ppermute | solution.py:22
  35.3 42.6 %collective-permute-start.10 = (bf16[1,32,3584]{2,1,0:T(8,128)(2,1)S(1)}, bf16[1,32,3584]{2,1,0:T(8,128)(2,1)S(1)}, u32[]{:S(2)}, u32[]{:S(2)}) collective-permute-start(bf16[1,32,3584]{2,1,0:T(8,128)(2,1)S(1)} %get-tuple-element.6), channel_id=1, source_target_pairs={{0,22},{2,20},{4,18},{6,16},{8,30},{10,28},{12,26},{14,24},{16,6},... | collective-permute-start | bytes 688136 | tf_op jit(solution)/shard_map/ppermute | solution.py:22
  40.2 47.5 %collective-permute-start.11 = (bf16[1,32,3584]{2,1,0:T(8,128)(2,1)S(1)}, bf16[1,32,3584]{2,1,0:T(8,128)(2,1)S(1)}, u32[]{:S(2)}, u32[]{:S(2)}) collective-permute-start(bf16[1,32,3584]{2,1,0:T(8,128)(2,1)S(1)} %get-tuple-element.5), channel_id=1, source_target_pairs={{0,24},{2,26},{4,28},{6,30},{8,16},{10,18},{12,20},{14,22},{16,8},... | collective-permute-start | bytes 688136 | tf_op jit(solution)/shard_map/ppermute | solution.py:22
  41.1 51.9 %collective-permute-start.12 = (bf16[1,32,3584]{2,1,0:T(8,128)(2,1)S(1)}, bf16[1,32,3584]{2,1,0:T(8,128)(2,1)S(1)}, u32[]{:S(2)}, u32[]{:S(2)}) collective-permute-start(bf16[1,32,3584]{2,1,0:T(8,128)(2,1)S(1)} %get-tuple-element.4), channel_id=1, source_target_pairs={{0,26},{2,24},{4,30},{6,28},{8,18},{10,16},{12,22},{14,20},{16,10}... | collective-permute-start | bytes 688136 | tf_op jit(solution)/shard_map/ppermute | solution.py:22
  63.2 34.4 %collective-permute-start.13 = (bf16[1,32,3584]{2,1,0:T(8,128)(2,1)S(1)}, bf16[1,32,3584]{2,1,0:T(8,128)(2,1)S(1)}, u32[]{:S(2)}, u32[]{:S(2)}) collective-permute-start(bf16[1,32,3584]{2,1,0:T(8,128)(2,1)S(1)} %get-tuple-element.3), channel_id=1, source_target_pairs={{0,28},{2,30},{4,24},{6,26},{8,20},{10,22},{12,16},{14,18},{16,12}... | collective-permute-start | bytes 688136 | tf_op jit(solution)/shard_map/ppermute | solution.py:22
  68.1 34.4 %collective-permute-start.14 = (bf16[1,32,3584]{2,1,0:T(8,128)(2,1)S(1)}, bf16[1,32,3584]{2,1,0:T(8,128)(2,1)S(1)}, u32[]{:S(2)}, u32[]{:S(2)}) collective-permute-start(bf16[1,32,3584]{2,1,0:T(8,128)(2,1)S(1)} %get-tuple-element.2), channel_id=1, source_target_pairs={{0,30},{2,28},{4,26},{6,24},{8,22},{10,20},{12,18},{14,16},{16,14}... | collective-permute-start | bytes 688136 | tf_op jit(solution)/shard_map/ppermute | solution.py:22
  102.5 2.1 copy-start.5
  104.6 2.2 copy-start.1
  111.9 6.3 %copy-start.3 = (f32[32,4]{0,1:T(4,128)S(1)}, f32[32,4]{0,1:T(4,128)}, u32[]{:S(2)}) copy-start(f32[32,4]{0,1:T(4,128)} %param.11) | copy-start | bytes 1540
  111.9 6.4 %copy-start.6 = (s32[4]{0:T(128)S(1)}, s32[4]{0:T(128)}, u32[]{:S(2)}) copy-start(s32[4]{0:T(128)} %param.17) | copy-start | bytes 52
  111.9 6.5 %copy-start.2 = (bf16[4,128,576]{1,2,0:T(8,128)(2,1)S(1)}, bf16[4,128,576]{1,2,0:T(8,128)(2,1)}, u32[]{:S(2)}) copy-start(bf16[4,128,576]{1,2,0:T(8,128)(2,1)} %param.16) | copy-start | bytes 1769476
  111.9 166.6 %all-to-all-start = ((f32[16,32,3584]{2,1,0:T(8,128)}), f32[16,32,3584]{2,1,0:T(8,128)}, u32[]{:S(2)}, u32[]{:S(2)}) async-start(f32[16,32,3584]{2,1,0:T(8,128)} %fusion.1), calls=%async_computation | async-start | bytes 14680064 | tf_op jit(solution)/shard_map/all_to_all | solution.py:73
